TPU v7x, 256 devices: a whole 4x4x8 slice. The times are simulated.
256 devices in a mesh: cfg: 2 (over core), req: 8 (over z), seq: 16 (over y, x).
Axes of the slice: x: 4, y: 4, z: 8, core: 2. Of those that a mesh axis runs over, the one named last changes fastest.
Arguments:
- img_hidden: bfloat16 [2, 16, 512, 1536], P('cfg', 'req', 'seq'), may hold values from -6 to 6
- txt_hidden: bfloat16 [2, 16, 160, 1536], P('cfg', 'req', 'seq'), may hold values from -6 to 6
- text_len: int32 [2, 16], P('cfg'), may hold values from 1 to 154, as said below
- pooled: float32 [2, 16, 1536], P('cfg'), may hold values from -6 to 6
- timestep: int32 [16], replicated, may hold values from 0 to 27
- latent: float32 [16, 512, 64], P('req', 'seq', 'cfg'), may hold values from -24 to 24
- mod_weight: bfloat16 [1536, 15360], P(None, ('req', 'seq')), may hold values from -0.15625 to 0.15625
- mod_bias: float32 [15360], P(('req', 'seq')), may hold values from -2 to 2
- img_qkv: bfloat16 [1536, 3, 1536], P(None, None, 'req'), may hold values from -2.5 to 2.5
- txt_kv: bfloat16 [1536, 2, 1536], P(None, None, 'req'), may hold values from -0.15625 to 0.15625
- out_weight: bfloat16 [1536, 1536], P('req'), may hold values from -0.15625 to 0.15625
- fc_in: bfloat16 [1536, 6144], P(None, 'seq'), may hold values from -0.15625 to 0.15625
- fc_out: bfloat16 [6144, 1536], P('seq'), may hold values from -0.078125 to 0.078125
- final_weight: bfloat16 [1536, 64], replicated, may hold values from -0.15625 to 0.15625
Outputs:
- velocity: float32 [16, 512, 64], P('req', 'seq', 'cfg')
- next_latent: float32 [16, 512, 64], P('req', 'seq', 'cfg')
- latent_norm: float32 [16], P('req')
- latent_peak: float32 [16], P('req')
Inputs may be any that keep to these rules, and one draw needn't show every extreme that they name: Text slots from text_len to 159 of a request are padding; every draw has a request of length 154 and one of length 1.
All inputs are finite; a program needn't handle non-finite values.
Results may differ from a plain program's by a relative error of at most 0.015.
Values may be sent and summed in bfloat16 or wider, within the bound.
No kernel may reach another device: no remote copies, remote signals or barrier semaphores. Data moves between devices by JAX's collectives and lax.ppermute only.
A program may use at most 64 MiB of HBM per device.

v0:
```python
import math
import jax
import jax.numpy as jnp
from jax import lax
from jax.sharding import PartitionSpec as P

D = 1536
HD = 64
PATCHC = 64
IMG = 512
STEPS = 28
SIGMA_SHIFT = 3.0
GUIDANCE = 5.0
EPSILON = 1e-06
MASKED_SCORE = -1e30


def from_partner(value, axis, distance):
    mask = 2**distance
    pairs = [(source, source ^ mask) for source in range(lax.axis_size(axis))]
    return lax.ppermute(value, axis, pairs)


def shifted(fraction):
    return SIGMA_SHIFT * fraction / (1.0 + (SIGMA_SHIFT - 1.0) * fraction)


def plan(timestep):
    position = timestep.astype(jnp.float32)
    return (shifted(1.0 - position / STEPS), shifted(1.0 - (position + 1.0) / STEPS))


def time_features(sigma):
    half_width = D // 2
    frequency = jnp.exp(-math.log(10000.0) * jnp.arange(half_width, dtype=jnp.float32) / half_width)
    angles = (1000.0 * sigma)[:, None] * frequency[None, :]
    return jnp.concatenate([jnp.cos(angles), jnp.sin(angles)], axis=1)


def layer_norm(values):
    average = jnp.mean(values, axis=-1, keepdims=True)
    centred = values - average
    spread = jnp.mean(centred * centred, axis=-1, keepdims=True)
    return centred * lax.rsqrt(spread + EPSILON)


def attention(queries, key_rows, value_rows, live_keys):
    query_count = queries.shape[0]
    head_count = queries.shape[1]
    block_rows = min(512, query_count)
    scale_factor = HD ** (-0.5)

    def one_block(query_block):
        scores = (
            jnp.einsum("qhd,khd->hqk", query_block, key_rows, preferred_element_type=jnp.float32)
            * scale_factor
        )
        scores = jnp.where(live_keys[None, None, :], scores, MASKED_SCORE)
        highest = jnp.max(scores, axis=-1, keepdims=True)
        exp_scores = jnp.exp(scores - highest)
        weights = (exp_scores / jnp.sum(exp_scores, axis=-1, keepdims=True)).astype(jnp.bfloat16)
        mixture = jnp.einsum(
            "hqk,khd->qhd", weights, value_rows, preferred_element_type=jnp.float32
        )
        return mixture.astype(jnp.bfloat16)

    blocks = queries.reshape(query_count // block_rows, block_rows, head_count, HD)
    return lax.map(one_block, blocks).reshape(query_count, head_count * HD)


def on_device(
    img_hidden,
    txt_hidden,
    text_len,
    pooled,
    timestep,
    latent,
    mod_weight,
    mod_bias,
    img_qkv,
    txt_kv,
    out_weight,
    fc_in,
    fc_out,
    final_weight,
):
    group_size = img_hidden.shape[1]
    current, upcoming = plan(timestep)
    activated = jax.nn.silu(pooled[0] + time_features(current)).astype(jnp.bfloat16)
    columns = jnp.dot(activated, mod_weight, preferred_element_type=jnp.float32) + mod_bias
    every_mod = lax.all_gather(columns, ("req", "seq"), axis=1, tiled=True)
    offset = lax.axis_index("req") * group_size
    modulation = lax.dynamic_slice_in_dim(every_mod, offset, group_size, 0).reshape(
        group_size, 10, 1, D
    )
    shift_attn, scale_attn, gate_attn = (modulation[:, 0], modulation[:, 1], modulation[:, 2])
    shift_mlp, scale_mlp, gate_mlp = (modulation[:, 3], modulation[:, 4], modulation[:, 5])
    shift_text, scale_text = (modulation[:, 6], modulation[:, 7])
    scale_final, shift_final = (modulation[:, 8], modulation[:, 9])
    img_float = img_hidden[0].astype(jnp.float32)
    img_in = (layer_norm(img_float) * (1.0 + scale_attn) + shift_attn).astype(jnp.bfloat16)
    txt_in = (
        layer_norm(txt_hidden[0].astype(jnp.float32)) * (1.0 + scale_text) + shift_text
    ).astype(jnp.bfloat16)
    all_img, all_txt = (
        lax.all_gather(img_in, "req", axis=0, tiled=True),
        lax.all_gather(txt_in, "req", axis=0, tiled=True),
    )
    head_width = img_qkv.shape[2]
    local_heads = head_width // HD
    qkv_columns = img_qkv.reshape(D, 3 * head_width)
    kv_columns = txt_kv.reshape(D, 2 * head_width)
    own_img, own_txt = (
        lax.all_to_all(all_img, "seq", split_axis=0, concat_axis=1, tiled=True),
        lax.all_to_all(all_txt, "seq", split_axis=0, concat_axis=1, tiled=True),
    )
    own_proj = jnp.einsum(
        "rnd,dc->rnc", own_img, qkv_columns, preferred_element_type=jnp.float32
    ).astype(jnp.bfloat16)
    own_proj_txt = jnp.einsum(
        "rnd,dc->rnc", own_txt, kv_columns, preferred_element_type=jnp.float32
    ).astype(jnp.bfloat16)
    local_count = own_proj.shape[0]
    image_rows = own_proj.shape[1]
    text_rows = own_proj_txt.shape[1]
    first_request = lax.axis_index("seq") * local_count

    def attend_request(operands):
        projected, projected_txt, request_slot = operands
        queries = projected[:, :head_width]
        key_rows = jnp.concatenate(
            [projected[:, head_width : 2 * head_width], projected_txt[:, :head_width]], axis=0
        )
        value_rows = jnp.concatenate(
            [projected[:, 2 * head_width :], projected_txt[:, head_width:]], axis=0
        )
        text_count = lax.dynamic_index_in_dim(text_len[0], first_request + request_slot, 0, False)
        live_keys = jnp.arange(image_rows + text_rows, dtype=jnp.int32) < image_rows + text_count
        total_keys = image_rows + text_rows
        return attention(
            queries.reshape(image_rows, local_heads, HD),
            key_rows.reshape(total_keys, local_heads, HD),
            value_rows.reshape(total_keys, local_heads, HD),
            live_keys,
        )

    attended = lax.map(
        attend_request, (own_proj, own_proj_txt, jnp.arange(local_count, dtype=jnp.int32))
    )
    projected_rows = jnp.einsum(
        "rnk,kd->rnd", attended, out_weight, preferred_element_type=jnp.float32
    )
    moved_rows = lax.all_to_all(
        projected_rows.astype(jnp.bfloat16), "seq", split_axis=1, concat_axis=0, tiled=True
    ).astype(projected_rows.dtype)
    attn_out = lax.psum_scatter(
        moved_rows.astype(jnp.bfloat16), "req", scatter_dimension=0, tiled=True
    ).astype(jnp.float32)
    img_mid = img_float + gate_attn * attn_out
    mlp_in = (layer_norm(img_mid) * (1.0 + scale_mlp) + shift_mlp).astype(jnp.bfloat16)
    raised = jnp.einsum(
        "rnd,df->rnf",
        lax.all_gather(mlp_in, "seq", axis=1, tiled=True),
        fc_in,
        preferred_element_type=jnp.float32,
    )
    hidden = jax.nn.gelu(raised, approximate=True).astype(jnp.bfloat16)
    mlp_terms = jnp.einsum("rnf,fd->rnd", hidden, fc_out, preferred_element_type=jnp.float32)
    mlp_out = lax.psum_scatter(
        mlp_terms.astype(jnp.bfloat16), "seq", scatter_dimension=1, tiled=True
    ).astype(jnp.float32)
    img_out = img_mid + gate_mlp * mlp_out
    final_in = (layer_norm(img_out) * (1.0 + scale_final) + shift_final).astype(jnp.bfloat16)
    own_velocity = jnp.einsum(
        "rnd,dc->rnc", final_in, final_weight, preferred_element_type=jnp.float32
    )
    half_values = latent.shape[2]
    half_index = lax.axis_index("cfg")
    kept_velocity = lax.dynamic_slice_in_dim(own_velocity, half_index * half_values, half_values, 2)
    sent_velocity = lax.dynamic_slice_in_dim(
        own_velocity, (1 - half_index) * half_values, half_values, 2
    )
    other_velocity = from_partner(sent_velocity, "cfg", 0)
    cond_first = half_index == 0
    conditional = jnp.where(cond_first, kept_velocity, other_velocity)
    unconditional = jnp.where(cond_first, other_velocity, kept_velocity)
    guided = unconditional + GUIDANCE * (conditional - unconditional)
    step_size = lax.dynamic_slice_in_dim(upcoming - current, offset, group_size, 0)
    next_latent = latent + step_size[:, None, None] * guided
    squares = jnp.sum(next_latent * next_latent, axis=(1, 2))
    largest = jnp.max(jnp.abs(next_latent), axis=(1, 2))
    square_total = lax.psum(squares, ("cfg", "seq"))
    peak_value = lax.pmax(largest, ("cfg", "seq"))
    latent_norm = jnp.sqrt(square_total / (IMG * PATCHC))
    return (guided, next_latent, latent_norm, peak_value)


def solution(mesh):
    placed = (
        P("cfg", "req", "seq", None),
        P("cfg", "req", "seq", None),
        P("cfg", None),
        P("cfg", None, None),
        P(),
        P("req", "seq", "cfg"),
        P(None, ("req", "seq")),
        P(("req", "seq")),
        P(None, None, "req"),
        P(None, None, "req"),
        P("req", None),
        P(None, "seq"),
        P("seq", None),
        P(),
    )
    return jax.shard_map(
        on_device,
        mesh=mesh,
        in_specs=placed,
        out_specs=(P("req", "seq", "cfg"), P("req", "seq", "cfg"), P("req"), P("req")),
        check_vma=False,
    )
```

profile of v0, /device:TPU:1, one launch (start us, length us, event | category | flops | bytes accessed | tf_op | source)
XLA Modules:
  0.0 808.6 jit_solution(5461950614559532431)
XLA Ops:
  8.3 1.2 fusion.18
  9.5 299.6 %all-gather = f32[128,120,16]{1,2,0:T(8,128)S(1)} all-gather(f32[1,120,16]{1,2,0:T(8,128)S(1)} %fusion.18), channel_id=1, replica_groups=mesh['cfg'=2,'req'=8,'seq'=16] {'req','seq'}, dimensions={0}, use_global_device_ids=true | all-gather | bytes 990720 | tf_op jit(solution)/shard_map/all_gather | solution.py:91
  309.4 1.6 reshape.180
  311.0 1.1 dynamic-slice_bitcast_fusion
  314.5 19.9 %all_gather.14 = bf16[16,10,1536]{2,1,0:T(8,128)(2,1)S(1)} all-gather(bf16[2,10,1536]{2,1,0:T(8,128)(2,1)S(1)} %fusion.42), channel_id=1, replica_groups=mesh['cfg'=2,'req'=8,'seq'=16] {'req'}, dimensions={0}, use_global_device_ids=true | all-gather | bytes 552960 | tf_op jit(solution)/shard_map/all_gather | solution.py:107
  334.4 13.0 %all_to_all.30 = bf16[16,10,1536]{2,1,0:T(8,128)(2,1)S(1)} all-to-all(bf16[16,10,1536]{2,1,0:T(8,128)(2,1)S(1)} %all_gather.14), channel_id=1, replica_groups=mesh['cfg'=2,'req'=8,'seq'=16] {'seq'}, dimensions={0} | all-to-all | bytes 983040 | tf_op jit(solution)/shard_map/all_to_all | solution.py:115
  347.4 51.1 %all-gather.4.cloned.1.call-done = bf16[16,32,1536]{2,1,0:T(8,128)(2,1)} async-done(((bf16[2,32,1536]{2,1,0:T(8,128)(2,1)}), bf16[16,32,1536]{2,1,0:T(8,128)(2,1)}) %all-gather.4.cloned.1.call-update) | async-done | bytes 1572880 | tf_op jit(solution)/shard_map/all_gather | solution.py:106
  398.5 5.8 all-to-all-start
  406.0 1.7 convolution_convert_fusion.3
  407.8 13.1 %all-to-all-done = bf16[16,32,1536]{2,1,0:T(8,128)(2,1)} async-done(((bf16[16,32,1536]{2,1,0:T(8,128)(2,1)}), bf16[16,32,1536]{2,1,0:T(8,128)(2,1)}, u32[]{:S(2)}, u32[]{:S(2)}) %all-to-all-start) | async-done | bytes 1572896 | tf_op jit(solution)/shard_map/all_to_all | solution.py:114
  420.9 2.5 convolution_convert_fusion.2
  423.5 3.5 fusion.63
  427.1 2.7 fusion.17
  430.4 4.1 copy.58
  435.0 11.5 %reduce.2 = bf16[512,1536]{1,0:T(8,128)(2,1)S(1)} reduce(bf16[512,1,1536]{2,1,0:T(2,128)(2,1)} %bitcast.126, bf16[]{:T(256)} %broadcast.203), dimensions={1}, to_apply=%bitcast.124.reduce_sub_computation | reduce | bytes 3145730
  446.5 2.1 reshape.184
  448.6 18.4 %all_to_all.31 = bf16[16,2,24576]{2,1,0:T(2,128)(2,1)S(1)} all-to-all(bf16[16,2,24576]{2,1,0:T(2,128)(2,1)} %reshape.184), channel_id=1, replica_groups=mesh['cfg'=2,'req'=8,'seq'=16] {'seq'}, dimensions={0} | all-to-all | bytes 3145728 | tf_op jit(solution)/shard_map/all_to_all | solution.py:153
  466.9 6.3 reshape.185
  473.2 3.4 copy.36
  477.3 42.2 %reduce-scatter.3.cloned.1.call-done = bf16[2,32,1536]{2,1,0:T(8,128)(2,1)} async-done(((bf16[16,32,1536]{2,1,0:T(8,128)(2,1)}), bf16[2,32,1536]{2,1,0:T(8,128)(2,1)}) %reduce-scatter.3.cloned.1.call-update) | async-done | bytes 196624 | tf_op jit(solution)/shard_map/reduce_scatter | solution.py:156
  519.5 1.1 fusion.35
  520.5 1.1 multiply_reduce_fusion.1
  521.7 1.8 add_convert_fusion.1
  523.5 54.8 %all-gather.6.cloned.1.call-done = bf16[2,512,1536]{2,1,0:T(8,128)(2,1)} async-done(((bf16[2,32,1536]{2,1,0:T(8,128)(2,1)}), bf16[2,512,1536]{2,1,0:T(8,128)(2,1)}) %all-gather.6.cloned.1.call-update) | async-done | bytes 3145744 | tf_op jit(solution)/shard_map/all_gather | solution.py:163
  578.4 7.6 convolution_convert_fusion
  586.6 78.8 %reduce-scatter.5.cloned.1.call-done = bf16[2,32,1536]{2,1,0:T(8,128)(2,1)} async-done(((bf16[2,512,1536]{2,1,0:T(8,128)(2,1)}), bf16[2,32,1536]{2,1,0:T(8,128)(2,1)}) %reduce-scatter.5.cloned.1.call-update) | async-done | bytes 196624 | tf_op jit(solution)/shard_map/reduce_scatter | solution.py:169
  665.5 1.1 fusion.58
  666.6 1.1 multiply_reduce_fusion
  667.8 1.2 fusion.43
  669.1 2.4 collective-permute-start
  673.1 65.3 %psum.7 = f32[2]{0:T(128)S(1)} all-reduce(f32[2]{0:T(128)S(1)} %get-tuple-element.41), channel_id=1, replica_groups=mesh['cfg'=2,'req'=8,'seq'=16] {'cfg','seq'}, use_global_device_ids=true, to_apply=%region_13.14 | all-reduce | flops 2 | bytes 16 | tf_op jit(solution)/shard_map/psum | solution.py:192
  738.8 63.2 %pmax.7 = f32[2]{0:T(128)} all-reduce(f32[2]{0:T(128)S(1)} %get-tuple-element.40), channel_id=1, replica_groups=mesh['cfg'=2,'req'=8,'seq'=16] {'cfg','seq'}, use_global_device_ids=true, to_apply=%region_15.16 | all-reduce | flops 2 | bytes 16 | tf_op jit(solution)/shard_map/pmax | solution.py:193
  (77 shorter events, 10.4 us)
Async XLA Ops:
  7.2 413.7 %copy-start = (bf16[1536,3,192]{0,2,1:T(8,128)(2,1)S(1)}, bf16[1536,3,192]{0,2,1:T(8,128)(2,1)}, u32[]{:S(2)}) copy-start(bf16[1536,3,192]{0,2,1:T(8,128)(2,1)} %param.22) | copy-start | bytes 5308420
  7.2 391.3 %all-gather.4.cloned.1.call-start = ((), (), s32[]{:S(2)}) async-start(), calls=%async_computation.5 | async-start | bytes 1769472 | tf_op jit(solution)/shard_map/all_gather | solution.py:106
  309.4 3.5 copy-start.1
  309.4 4.7 copy-start.4
  347.4 57.1 %copy-start.13 = (s32[1,16]{1,0:T(1,128)S(1)}, s32[1,16]{1,0:T(1,128)}, u32[]{:S(2)}) copy-start(s32[1,16]{1,0:T(1,128)} %param.16) | copy-start | bytes 196
  398.5 22.4 %all-to-all-start = ((bf16[16,32,1536]{2,1,0:T(8,128)(2,1)}), bf16[16,32,1536]{2,1,0:T(8,128)(2,1)}, u32[]{:S(2)}, u32[]{:S(2)}) async-start(bf16[16,32,1536]{2,1,0:T(8,128)(2,1)} %all-gather.4.cloned.1.call-done), calls=%async_computation | async-start | bytes 3145728 | tf_op jit(solution)/shard_map/all_to_all | solution.py:114
  404.3 115.1 %reduce-scatter.3.cloned.1.call-start = ((), (), s32[]{:S(2)}) async-start(), calls=%async_computation.6 | async-start | bytes 1769472 | tf_op jit(solution)/shard_map/reduce_scatter | solution.py:156
  427.1 2.7 copy-start.3
  476.5 0.7 copy-start.5
  476.5 0.7 copy-start.8
  476.5 0.7 copy-start.9
  476.5 101.8 %copy-start.11 = (bf16[384,1536]{1,0:T(8,128)(2,1)S(1)}, bf16[384,1536]{1,0:T(8,128)(2,1)}, u32[]{:S(2)}) copy-start(bf16[384,1536]{1,0:T(8,128)(2,1)} %param.26) | copy-start | bytes 3538948
  476.6 101.8 %all-gather.6.cloned.1.call-start = ((), (), s32[]{:S(2)}) async-start(), calls=%async_computation.7 | async-start | bytes 3342336 | tf_op jit(solution)/shard_map/all_gather | solution.py:163
  523.5 142.0 %reduce-scatter.5.cloned.1.call-start = ((), (), s32[]{:S(2)}) async-start(), calls=%async_computation.8 | async-start | bytes 3342336 | tf_op jit(solution)/shard_map/reduce_scatter | solution.py:169
  585.9 0.7 copy-start.6
  585.9 0.7 copy-start.7
  585.9 79.6 %copy-start.2 = (bf16[2,32,1536]{2,1,0:T(8,128)(2,1)S(1)}, bf16[2,32,1536]{2,1,0:T(8,128)(2,1)}, u32[]{:S(2)}) copy-start(bf16[2,32,1536]{2,1,0:T(8,128)(2,1)} %reduce-scatter.3.cloned.1.call-done) | copy-start | bytes 589828
  585.9 81.9 %copy-start.12 = (bf16[1536,64]{0,1:T(8,128)(2,1)S(1)}, bf16[1536,64]{0,1:T(8,128)(2,1)}, u32[]{:S(2)}) copy-start(bf16[1536,64]{0,1:T(8,128)(2,1)} %param.27) | copy-start | bytes 589828
  585.9 86.4 %copy-start.10 = (f32[2,32,32]{2,1,0:T(8,128)S(1)}, f32[2,32,32]{2,1,0:T(8,128)}, u32[]{:S(2)}) copy-start(f32[2,32,32]{2,1,0:T(8,128)} %param.19) | copy-start | bytes 24580
  669.1 3.3 collective-permute-start
Sparse Core Ops, SparseCore 0:
  314.2 84.2 all-gather.3
  476.7 42.7 reduce-scatter.2
  523.6 54.7 all-gather.5
  586.1 79.3 reduce-scatter.4
where the time goes:
time: 809 us
  blocking collectives  479 us (59%)
  waiting for transfers between devices  241 us (30%)
  other arithmetic  23.5 us (3%)
  local copies, waits for them, and re-layouts  21.2 us (3%)
  matrix products  21.1 us (3%)
  between operations  14 us (2%)
  starting transfers between devices  8.55 us (1%)
    all_gather x1, blocking collectives, on_device(): every_mod = lax.all_gather(columns, ('req', 'seq'), axis=1, tiled=True)  300 us
    reduce_scatter x1, waiting for transfers between devices, on_device(): lax.psum_scatter(mlp_terms.astype(jnp.bfloat16), 'seq', scatter_dimension...  78.8 us
    psum x1, blocking collectives, on_device(): square_total = lax.psum(squares, ('cfg', 'seq'))  65.3 us
    pmax x1, blocking collectives, on_device(): peak_value = lax.pmax(largest, ('cfg', 'seq'))  63.2 us
    all_gather x1, waiting for transfers between devices, on_device(): lax.all_gather(mlp_in, 'seq', axis=1, tiled=True)  54.8 us
    all_gather x1, waiting for transfers between devices, on_device(): lax.all_gather(img_in, 'req', axis=0, tiled=True)  51.1 us
    reduce_scatter x1, waiting for transfers between devices, on_device(): lax.psum_scatter(moved_rows.astype(jnp.bfloat16), 'req', scatter_dimensio...  42.2 us
    all_gather x1, blocking collectives, on_device(): lax.all_gather(txt_in, 'req', axis=0, tiled=True)  19.9 us
  transfers between devices with their start and end apart: 6, of which 6 were waited for; matrix products, arithmetic and copies ran while one was open for 0% of the time, Pallas kernels for 0%

commit v1 on v0

--- a/solution.py
+++ b/solution.py
@@ -13,6 +13,28 @@
 GUIDANCE = 5.0
 EPSILON = 1e-06
 MASKED_SCORE = -1e30
+
+
+def in_order(blocks, dim):
+    dims = list(blocks.shape[1:])
+    dims[dim] *= blocks.shape[0]
+    return jnp.moveaxis(blocks, 0, dim).reshape(dims)
+
+
+def ring_gather(x, axis, dim):
+    size = lax.axis_size(axis)
+    pairs = [(i, (i + 1) % size) for i in range(size)]
+    back = [(b, a) for a, b in pairs]
+    lower, upper = ([], [])
+    for step in range(size - 1):
+        if step % 2 == 0:
+            lower.append(lax.ppermute(lower[-1] if lower else x, axis, pairs))
+        else:
+            upper.append(lax.ppermute(upper[-1] if upper else x, axis, back))
+    blocks = jnp.stack([*lower[::-1], x, *upper])
+    shift = lax.axis_index(axis) - len(lower)
+    blocks = blocks[(jnp.arange(size) - shift) % size]
+    return in_order(blocks, dim)
 
 
 def from_partner(value, axis, distance):
@@ -159,10 +181,7 @@
     img_mid = img_float + gate_attn * attn_out
     mlp_in = (layer_norm(img_mid) * (1.0 + scale_mlp) + shift_mlp).astype(jnp.bfloat16)
     raised = jnp.einsum(
-        "rnd,df->rnf",
-        lax.all_gather(mlp_in, "seq", axis=1, tiled=True),
-        fc_in,
-        preferred_element_type=jnp.float32,
+        "rnd,df->rnf", ring_gather(mlp_in, "seq", 1), fc_in, preferred_element_type=jnp.float32
     )
     hidden = jax.nn.gelu(raised, approximate=True).astype(jnp.bfloat16)
     mlp_terms = jnp.einsum("rnf,fd->rnd", hidden, fc_out, preferred_element_type=jnp.float32)

time: 809 us -> 857 us (1.059)
  starting transfers between devices: 8.55 us -> 44.6 us
  local copies, waits for them, and re-layouts: 21.2 us -> 44.7 us
  waiting for transfers between devices: 241 us -> 226 us
    all_gather x1 -> x0, waiting for transfers between devices: 54.8 us -> none  [on_device(): lax.all_gather(mlp_in, 'seq', axis=1, tiled=True)]
    ppermute x0 -> x15, starting transfers between devices: none -> 35.8 us  [the longest x7 34.3 us: ring_gather(): upper.append(lax.ppermute(upper[-1] if upper else x, axis, back))]
    ppermute x0 -> x15, waiting for transfers between devices: none -> 32.9 us  [the longest x8 32.8 us: ring_gather(): lower.append(lax.ppermute(lower[-1] if lower else x, axis, pairs))]
    unnamed x39 -> x60, local copies, waits for them, and re-layouts: 15.2 us -> 29.7 us
  transfers between devices with their start and end apart: 6 -> 20, of which waited for: 6 -> 14; matrix products, arithmetic and copies ran while one was open for 0% -> 2% of each run, Pallas kernels for 0% -> 0%
where the time goes in v1:
time: 857 us; the launch traced here: 854 us
  blocking collectives  479 us (56%)
  waiting for transfers between devices  226 us (26%)
  local copies, waits for them, and re-layouts  44.7 us (5%)
  starting transfers between devices  44.6 us (5%)
  other arithmetic  23.3 us (3%)
  matrix products  21 us (2%)
  between operations  14.3 us (2%)
    all_gather x1, blocking collectives, on_device(): every_mod = lax.all_gather(columns, ('req', 'seq'), axis=1, tiled=True)  300 us
    reduce_scatter x1, waiting for transfers between devices, on_device(): lax.psum_scatter(mlp_terms.astype(jnp.bfloat16), 'seq', scatter_dimension...  86 us
    psum x1, blocking collectives, on_device(): square_total = lax.psum(squares, ('cfg', 'seq'))  65.3 us
    pmax x1, blocking collectives, on_device(): peak_value = lax.pmax(largest, ('cfg', 'seq'))  63.2 us
    all_gather x1, waiting for transfers between devices, on_device(): lax.all_gather(img_in, 'req', axis=0, tiled=True)  51 us
    reduce_scatter x1, waiting for transfers between devices, on_device(): lax.psum_scatter(moved_rows.astype(jnp.bfloat16), 'req', scatter_dimensio...  42.7 us
    ppermute x7, starting transfers between devices, ring_gather(): upper.append(lax.ppermute(upper[-1] if upper else x, axis, back))  34.3 us
    ppermute x8, waiting for transfers between devices, ring_gather(): lower.append(lax.ppermute(lower[-1] if lower else x, axis, pairs))  32.8 us
  transfers between devices with their start and end apart: 20, of which 14 were waited for; matrix products, arithmetic and copies ran while one was open for 2% of the time, Pallas kernels for 0%

profile of v1, /device:TPU:1, one launch (start us, length us, event | category | flops | bytes accessed | tf_op | source)
XLA Modules:
  0.0 853.5 jit_solution(12414763235953717062)
XLA Ops:
  10.0 299.7 %all-gather = f32[128,120,16]{1,2,0:T(8,128)S(1)} all-gather(f32[1,120,16]{1,2,0:T(8,128)S(1)} %fusion.18), channel_id=1, replica_groups=mesh['cfg'=2,'req'=8,'seq'=16] {'req','seq'}, dimensions={0}, use_global_device_ids=true | all-gather | bytes 990720 | tf_op jit(solution)/shard_map/all_gather | solution.py:113
  315.2 19.9 %all_gather.11 = bf16[16,10,1536]{2,1,0:T(8,128)(2,1)S(1)} all-gather(bf16[2,10,1536]{2,1,0:T(8,128)(2,1)S(1)} %fusion.42), channel_id=1, replica_groups=mesh['cfg'=2,'req'=8,'seq'=16] {'req'}, dimensions={0}, use_global_device_ids=true | all-gather | bytes 552960 | tf_op jit(solution)/shard_map/all_gather | solution.py:129
  335.1 13.0 %all_to_all.30 = bf16[16,10,1536]{2,1,0:T(8,128)(2,1)S(1)} all-to-all(bf16[16,10,1536]{2,1,0:T(8,128)(2,1)S(1)} %all_gather.11), channel_id=1, replica_groups=mesh['cfg'=2,'req'=8,'seq'=16] {'seq'}, dimensions={0} | all-to-all | bytes 983040 | tf_op jit(solution)/shard_map/all_to_all | solution.py:137
  348.1 51.0 %all-gather.3.cloned.1.call-done = bf16[16,32,1536]{2,1,0:T(8,128)(2,1)} async-done(((bf16[2,32,1536]{2,1,0:T(8,128)(2,1)}), bf16[16,32,1536]{2,1,0:T(8,128)(2,1)}) %all-gather.3.cloned.1.call-update) | async-done | bytes 1572880 | tf_op jit(solution)/shard_map/all_gather | solution.py:128
  399.1 5.9 all-to-all-start
  408.7 12.7 %all-to-all-done = bf16[16,32,1536]{2,1,0:T(8,128)(2,1)} async-done(((bf16[16,32,1536]{2,1,0:T(8,128)(2,1)}), bf16[16,32,1536]{2,1,0:T(8,128)(2,1)}, u32[]{:S(2)}, u32[]{:S(2)}) %all-to-all-start) | async-done | bytes 1572896 | tf_op jit(solution)/shard_map/all_to_all | solution.py:136
  424.0 3.5 fusion.65
  430.9 4.1 copy.61
  435.5 11.4 %reduce.2 = bf16[512,1536]{1,0:T(8,128)(2,1)S(1)} reduce(bf16[512,1,1536]{2,1,0:T(2,128)(2,1)} %bitcast.162, bf16[]{:T(256)} %broadcast.272), dimensions={1}, to_apply=%bitcast.160.reduce_sub_computation | reduce | bytes 3145730
  449.0 18.4 %all_to_all.31 = bf16[16,2,24576]{2,1,0:T(2,128)(2,1)S(1)} all-to-all(bf16[16,2,24576]{2,1,0:T(2,128)(2,1)} %reshape.245), channel_id=1, replica_groups=mesh['cfg'=2,'req'=8,'seq'=16] {'seq'}, dimensions={0} | all-to-all | bytes 3145728 | tf_op jit(solution)/shard_map/all_to_all | solution.py:175
  467.3 6.3 reshape.246
  473.6 3.4 copy.39
  477.2 42.7 %reduce-scatter.3.cloned.1.call-done = bf16[2,32,1536]{2,1,0:T(8,128)(2,1)} async-done(((bf16[16,32,1536]{2,1,0:T(8,128)(2,1)}), bf16[2,32,1536]{2,1,0:T(8,128)(2,1)}) %reduce-scatter.3.cloned.1.call-update) | async-done | bytes 196624 | tf_op jit(solution)/shard_map/reduce_scatter | solution.py:178
  524.4 6.7 collective-permute-done
  531.0 4.8 collective-permute-start.8
  538.9 4.8 collective-permute-start.9
  543.7 3.4 collective-permute-done.2
  547.1 5.1 collective-permute-start.10
  552.1 4.3 collective-permute-done.3
  556.5 5.2 collective-permute-start.11
  561.8 4.4 collective-permute-done.4
  566.4 4.8 collective-permute-start.12
  571.2 4.2 collective-permute-done.5
  575.4 4.8 collective-permute-start.13
  580.1 3.7 collective-permute-done.6
  583.9 4.9 collective-permute-start.14
  607.7 4.3 gather_fusion
  612.0 4.0 copy.32
  616.0 7.5 convolution_convert_fusion
  624.3 86.0 %reduce-scatter.5.cloned.1.call-done = bf16[2,32,1536]{2,1,0:T(8,128)(2,1)} async-done(((bf16[2,512,1536]{2,1,0:T(8,128)(2,1)}), bf16[2,32,1536]{2,1,0:T(8,128)(2,1)}) %reduce-scatter.5.cloned.1.call-update) | async-done | bytes 196624 | tf_op jit(solution)/shard_map/reduce_scatter | solution.py:188
  717.8 65.3 %psum.7 = f32[2]{0:T(128)S(1)} all-reduce(f32[2]{0:T(128)S(1)} %get-tuple-element.41), channel_id=1, replica_groups=mesh['cfg'=2,'req'=8,'seq'=16] {'cfg','seq'}, use_global_device_ids=true, to_apply=%region_13.14 | all-reduce | flops 2 | bytes 16 | tf_op jit(solution)/shard_map/psum | solution.py:211
  783.6 63.2 %pmax.7 = f32[2]{0:T(128)} all-reduce(f32[2]{0:T(128)S(1)} %get-tuple-element.40), channel_id=1, replica_groups=mesh['cfg'=2,'req'=8,'seq'=16] {'cfg','seq'}, use_global_device_ids=true, to_apply=%region_15.16 | all-reduce | flops 2 | bytes 16 | tf_op jit(solution)/shard_map/pmax | solution.py:212
  (130 shorter events, 56.2 us)
Async XLA Ops:
  7.2 414.2 %copy-start = (bf16[1536,3,192]{0,2,1:T(8,128)(2,1)S(1)}, bf16[1536,3,192]{0,2,1:T(8,128)(2,1)}, u32[]{:S(2)}) copy-start(bf16[1536,3,192]{0,2,1:T(8,128)(2,1)} %param.22) | copy-start | bytes 5308420
  7.2 391.9 %all-gather.3.cloned.1.call-start = ((), (), s32[]{:S(2)}) async-start(), calls=%async_computation.5 | async-start | bytes 1769472 | tf_op jit(solution)/shard_map/all_gather | solution.py:128
  10.0 303.5 %copy-start.1 = (bf16[1,2,32,1536]{3,2,1,0:T(8,128)(2,1)S(1)}, bf16[1,2,32,1536]{3,2,1,0:T(8,128)(2,1)}, u32[]{:S(2)}) copy-start(bf16[1,2,32,1536]{3,2,1,0:T(8,128)(2,1)} %param.14) | copy-start | bytes 589828
  309.7 5.0 copy-start.4
  314.7 90.8 %copy-start.15 = (s32[1,16]{1,0:T(1,128)S(1)}, s32[1,16]{1,0:T(1,128)}, u32[]{:S(2)}) copy-start(s32[1,16]{1,0:T(1,128)} %param.16) | copy-start | bytes 196
  399.1 22.3 %all-to-all-start = ((bf16[16,32,1536]{2,1,0:T(8,128)(2,1)}), bf16[16,32,1536]{2,1,0:T(8,128)(2,1)}, u32[]{:S(2)}, u32[]{:S(2)}) async-start(bf16[16,32,1536]{2,1,0:T(8,128)(2,1)} %all-gather.3.cloned.1.call-done), calls=%async_computation | async-start | bytes 3145728 | tf_op jit(solution)/shard_map/all_to_all | solution.py:136
  405.0 114.8 %reduce-scatter.3.cloned.1.call-start = ((), (), s32[]{:S(2)}) async-start(), calls=%async_computation.6 | async-start | bytes 1769472 | tf_op jit(solution)/shard_map/reduce_scatter | solution.py:178
  473.6 3.5 copy-start.11
  477.1 233.2 %reduce-scatter.5.cloned.1.call-start = ((), (), s32[]{:S(2)}) async-start(), calls=%async_computation.7 | async-start | bytes 3342336 | tf_op jit(solution)/shard_map/reduce_scatter | solution.py:188
  523.1 7.9 collective-permute-start
  531.0 7.8 collective-permute-start.1
  531.0 7.8 collective-permute-start.8
  538.9 8.2 collective-permute-start.2
  538.9 8.2 collective-permute-start.9
  547.1 9.3 %collective-permute-start.3 = (bf16[2,32,1536]{2,1,0:T(8,128)(2,1)S(1)}, bf16[2,32,1536]{2,1,0:T(8,128)(2,1)S(1)}, u32[]{:S(2)}, u32[]{:S(2)}) collective-permute-start(bf16[2,32,1536]{2,1,0:T(8,128)(2,1)S(1)} %collective-permute-done.2), channel_id=1, source_target_pairs={{0,1},{1,2},{2,3},{3,4},{4,5},{5,6},{6,7},{7,8},{8,9},{9,10},{10,1... | collective-permute-start | bytes 589832 | tf_op jit(solution)/shard_map/ppermute | solution.py:31
  547.1 9.5 %collective-permute-start.10 = (bf16[2,32,1536]{2,1,0:T(8,128)(2,1)S(1)}, bf16[2,32,1536]{2,1,0:T(8,128)(2,1)S(1)}, u32[]{:S(2)}, u32[]{:S(2)}) collective-permute-start(bf16[2,32,1536]{2,1,0:T(8,128)(2,1)S(1)} %collective-permute-done.9), channel_id=1, source_target_pairs={{1,0},{2,1},{3,2},{4,3},{5,4},{6,5},{7,6},{8,7},{9,8},{10,9},{11,1... | collective-permute-start | bytes 589832 | tf_op jit(solution)/shard_map/ppermute | solution.py:33
  556.4 9.9 %copy-start.5 = (bf16[2,32,1536]{2,1,0:T(8,128)(2,1)}, bf16[2,32,1536]{2,1,0:T(8,128)(2,1)S(1)}, u32[]{:S(2)}) copy-start(bf16[2,32,1536]{2,1,0:T(8,128)(2,1)S(1)} %collective-permute-done.3) | copy-start | bytes 589828
  556.4 9.7 %collective-permute-start.4 = (bf16[2,32,1536]{2,1,0:T(8,128)(2,1)S(1)}, bf16[2,32,1536]{2,1,0:T(8,128)(2,1)S(1)}, u32[]{:S(2)}, u32[]{:S(2)}) collective-permute-start(bf16[2,32,1536]{2,1,0:T(8,128)(2,1)S(1)} %collective-permute-done.3), channel_id=1, source_target_pairs={{0,1},{1,2},{2,3},{3,4},{4,5},{5,6},{6,7},{7,8},{8,9},{9,10},{10,1... | collective-permute-start | bytes 589832 | tf_op jit(solution)/shard_map/ppermute | solution.py:31
  556.5 9.8 %collective-permute-start.11 = (bf16[2,32,1536]{2,1,0:T(8,128)(2,1)S(1)}, bf16[2,32,1536]{2,1,0:T(8,128)(2,1)S(1)}, u32[]{:S(2)}, u32[]{:S(2)}) collective-permute-start(bf16[2,32,1536]{2,1,0:T(8,128)(2,1)S(1)} %collective-permute-done.10), channel_id=1, source_target_pairs={{1,0},{2,1},{3,2},{4,3},{5,4},{6,5},{7,6},{8,7},{9,8},{10,9},{11,1... | collective-permute-start | bytes 589832 | tf_op jit(solution)/shard_map/ppermute | solution.py:33
  566.1 5.1 copy-start.6
  566.1 9.2 %collective-permute-start.5 = (bf16[2,32,1536]{2,1,0:T(8,128)(2,1)S(1)}, bf16[2,32,1536]{2,1,0:T(8,128)(2,1)}, u32[]{:S(2)}, u32[]{:S(2)}) collective-permute-start(bf16[2,32,1536]{2,1,0:T(8,128)(2,1)S(1)} %collective-permute-done.4), channel_id=1, source_target_pairs={{0,1},{1,2},{2,3},{3,4},{4,5},{5,6},{6,7},{7,8},{8,9},{9,10},{10,1... | collective-permute-start | bytes 589832 | tf_op jit(solution)/shard_map/ppermute | solution.py:31
  566.4 9.0 %collective-permute-start.12 = (bf16[2,32,1536]{2,1,0:T(8,128)(2,1)S(1)}, bf16[2,32,1536]{2,1,0:T(8,128)(2,1)}, u32[]{:S(2)}, u32[]{:S(2)}) collective-permute-start(bf16[2,32,1536]{2,1,0:T(8,128)(2,1)S(1)} %collective-permute-done.11), channel_id=1, source_target_pairs={{1,0},{2,1},{3,2},{4,3},{5,4},{6,5},{7,6},{8,7},{9,8},{10,9},{11,1... | collective-permute-start | bytes 589832 | tf_op jit(solution)/shard_map/ppermute | solution.py:33
  575.4 8.5 collective-permute-start.6
  575.4 8.5 collective-permute-start.13
  583.9 8.1 collective-permute-start.7
  583.9 23.1 %collective-permute-start.14 = (bf16[2,32,1536]{2,1,0:T(8,128)(2,1)S(1)}, bf16[2,32,1536]{2,1,0:T(8,128)(2,1)S(1)}, u32[]{:S(2)}, u32[]{:S(2)}) collective-permute-start(bf16[2,32,1536]{2,1,0:T(8,128)(2,1)S(1)} %collective-permute-done.13), channel_id=1, source_target_pairs={{1,0},{2,1},{3,2},{4,3},{5,4},{6,5},{7,6},{8,7},{9,8},{10,9},{11,1... | collective-permute-start | bytes 589832 | tf_op jit(solution)/shard_map/ppermute | solution.py:33
  612.0 4.0 copy-start.13
  623.5 86.7 %copy-start.2 = (bf16[2,32,1536]{2,1,0:T(8,128)(2,1)S(1)}, bf16[2,32,1536]{2,1,0:T(8,128)(2,1)}, u32[]{:S(2)}) copy-start(bf16[2,32,1536]{2,1,0:T(8,128)(2,1)} %reduce-scatter.3.cloned.1.call-done) | copy-start | bytes 589828
  623.5 89.0 %copy-start.14 = (bf16[1536,64]{0,1:T(8,128)(2,1)S(1)}, bf16[1536,64]{0,1:T(8,128)(2,1)}, u32[]{:S(2)}) copy-start(bf16[1536,64]{0,1:T(8,128)(2,1)} %param.27) | copy-start | bytes 589828
  623.5 92.7 %copy-start.16 = (f32[16]{0:T(128)S(1)}, f32[16]{0:T(128)}, u32[]{:S(2)}) copy-start(f32[16]{0:T(128)} %get-tuple-element.50) | copy-start | bytes 196
  623.5 93.5 %copy-start.12 = (f32[2,32,32]{2,1,0:T(8,128)S(1)}, f32[2,32,32]{2,1,0:T(8,128)}, u32[]{:S(2)}) copy-start(f32[2,32,32]{2,1,0:T(8,128)} %param.19) | copy-start | bytes 24580
  713.8 3.2 collective-permute-start.15
  (5 other events, 8.4 us)
Sparse Core Ops, SparseCore 0:
  314.9 84.1 all-gather.2
  477.2 42.6 reduce-scatter.2
  623.7 86.4 reduce-scatter.4
